TPU v7x, 512 devices: a whole 4x8x8 slice. The times are simulated.
512 devices in a mesh: dp: 32 (over x, z_lo, core), ctx: 16 (over z_hi, y).
Axes of the slice: x: 4, y: 8, z: 8 (z_hi: 2, z_lo: 4; z = z_hi * 4 + z_lo), core: 2. Of those that a mesh axis runs over, the one named last changes fastest.
Arguments:
- queries: bfloat16 [32, 16, 128, 2048], P('dp', 'ctx'), may hold values from -2.5 to 2.5
- rotated_key_rows: bfloat16 [32, 16, 128, 512], P('dp', 'ctx'), may hold values from -2.5 to 2.5
- values: bfloat16 [32, 16, 128, 512], P('dp', 'ctx'), may hold values from -6 to 6
- cotangent: bfloat16 [32, 16, 128, 2048], P('dp', 'ctx'), may hold values from -6 to 6
- hidden: bfloat16 [32, 16, 128, 4096], P('dp', 'ctx'), may hold values from -6 to 6
- adapter_down_weight: bfloat16 [4096, 16], replicated, may hold values from -0.09375 to 0.09375
- adapter_up_weight: bfloat16 [16, 512], replicated, may hold values from -1.5 to 1.5
- segment_text_length: int32 [32, 16], P('dp', 'ctx'), may hold values from 19 to 78, as said below
Outputs:
- grad_queries: bfloat16 [32, 16, 128, 2048], P('dp', 'ctx')
- grad_keys: bfloat16 [32, 16, 128, 512], P('dp', 'ctx')
- grad_values: bfloat16 [32, 16, 128, 512], P('dp', 'ctx')
- grad_down: float32 [4096, 16], replicated
- grad_up: float32 [16, 512], replicated
Inputs may be any that keep to these rules, and one draw needn't show every extreme that they name: `segment_text_length`: every log has a segment with exactly 78 text tokens and another with the fewest.
All inputs are finite; a program needn't handle non-finite values.
Results may differ from a plain program's by a relative error of at most 0.0019.
The roundings to bfloat16 on the way count: a program that leaves them out, or rounds other values in their place, can miss the bound.
Values may be sent and summed in bfloat16 or wider, within the bound.
No kernel may reach another device: no remote copies, remote signals or barrier semaphores. Data moves between devices by JAX's collectives and lax.ppermute only.
A program may use at most 64 MiB of HBM per device.

v0:
```python
import math
import jax
import jax.numpy as jnp
from jax import lax
from jax.sharding import PartitionSpec as P

HEAD_SIZE = 128
SUMM = 50
adapter_scale = 2.0


def group_grads(query_group, key_group, value_group, cot_group, key_mask):
    softmax_scale = 1.0 / math.sqrt(HEAD_SIZE)
    scores = (
        jnp.einsum("tgd,md->gtm", query_group, key_group, preferred_element_type=jnp.float32)
        * softmax_scale
    )
    unnorm = jnp.exp(jnp.where(key_mask[None], scores, -jnp.inf))
    attend = unnorm / jnp.sum(unnorm, -1, keepdims=True)
    attend_grad = jnp.einsum(
        "tgd,md->gtm", cot_group, value_group, preferred_element_type=jnp.float32
    )
    row_dot = jnp.sum(attend * attend_grad, -1, keepdims=True)
    dscore = (attend * (attend_grad - row_dot)).astype(jnp.bfloat16)
    attend_low = attend.astype(jnp.bfloat16)
    query_grad = (
        jnp.einsum("gtm,md->tgd", dscore, key_group, preferred_element_type=jnp.float32)
        * softmax_scale
    )
    key_grad = (
        jnp.einsum("gtm,tgd->md", dscore, query_group, preferred_element_type=jnp.float32)
        * softmax_scale
    )
    value_grad = jnp.einsum(
        "gtm,tgd->md", attend_low, cot_group, preferred_element_type=jnp.float32
    )
    return (query_grad, key_grad, value_grad)


def adapter_terms(hidden_piece, low_rank_piece, value_piece, adapter_up_weight):
    contract = (((0,), (0,)), ((), ()))
    backward_step = lax.dot_general(
        value_piece, adapter_up_weight, (((1,), (1,)), ((), ())), preferred_element_type=jnp.float32
    ).astype(jnp.bfloat16)
    down_part = lax.dot_general(
        hidden_piece, backward_step, contract, preferred_element_type=jnp.float32
    )
    up_part = lax.dot_general(
        low_rank_piece, value_piece, contract, preferred_element_type=jnp.float32
    )
    return (down_part, up_part)


def per_device(
    queries,
    rotated_key_rows,
    values,
    cotangent,
    hidden,
    adapter_down_weight,
    adapter_up_weight,
    segment_text_length,
):
    query_rows = queries[0, 0]
    key_local = rotated_key_rows[0, 0]
    value_local = values[0, 0]
    cot_rows = cotangent[0, 0]
    hidden_row_block = hidden[0, 0]
    length = segment_text_length[0, 0]
    position = lax.axis_index("ctx")
    segment_list = lax.axis_size("ctx")
    log_batch = lax.axis_size("dp")
    tokens = query_rows.shape[0]
    width = key_local.shape[1]
    kv_heads = width // HEAD_SIZE
    groups = query_rows.shape[1] // width
    live = length + SUMM
    rows = jnp.arange(tokens)
    cot_rows = jnp.where((rows < live)[:, None], cot_rows, jnp.zeros_like(cot_rows))
    own_keys = lax.dynamic_slice_in_dim(key_local, length, SUMM, 0)
    own_values = lax.dynamic_slice_in_dim(value_local, length, SUMM, 0)
    memory_keys, memory_values = (
        lax.all_gather(own_keys, "ctx", axis=0, tiled=True),
        lax.all_gather(own_values, "ctx", axis=0, tiled=True),
    )
    count = memory_keys.shape[0]
    memory_owner = jnp.arange(count) // SUMM
    local_mask = (rows[None, :] <= rows[:, None]) & (rows[None, :] < live)
    memory_mask = jnp.broadcast_to((memory_owner < position)[None, :], (tokens, count))
    key_mask = jnp.concatenate([memory_mask, local_mask], axis=1)
    all_keys = jnp.concatenate([memory_keys, key_local], 0)
    all_values = jnp.concatenate([memory_values, value_local], 0)
    query_parts, key_parts, value_parts = ([], [], [])
    for group in range(kv_heads):
        qcols = slice(group * groups * HEAD_SIZE, (group + 1) * groups * HEAD_SIZE)
        kcols = slice(group * HEAD_SIZE, (group + 1) * HEAD_SIZE)
        query_grad, key_grad, value_grad = group_grads(
            query_rows[:, qcols].reshape(tokens, groups, HEAD_SIZE),
            all_keys[:, kcols],
            all_values[:, kcols],
            cot_rows[:, qcols].reshape(tokens, groups, HEAD_SIZE),
            key_mask,
        )
        query_parts.append(query_grad.reshape(tokens, groups * HEAD_SIZE))
        key_parts.append(key_grad)
        value_parts.append(value_grad)
    query_out = jnp.concatenate(query_parts, 1).astype(jnp.bfloat16)
    key_grad = jnp.concatenate(key_parts, 1)
    value_grad = jnp.concatenate(value_parts, 1)
    memory_key_grad, local_key = (key_grad[:count], key_grad[count:])
    memory_value_grad, local_value = (value_grad[:count], value_grad[count:])
    back_key, back_value = (
        lax.psum_scatter(memory_key_grad, "ctx", scatter_dimension=0, tiled=True),
        lax.psum_scatter(memory_value_grad, "ctx", scatter_dimension=0, tiled=True),
    )
    key_out = (
        local_key + lax.dynamic_update_slice_in_dim(jnp.zeros_like(local_key), back_key, length, 0)
    ).astype(jnp.bfloat16)
    value_result = (
        local_value
        + lax.dynamic_update_slice_in_dim(jnp.zeros_like(local_value), back_value, length, 0)
    ).astype(jnp.bfloat16)
    low_rank_rows = jnp.dot(
        hidden_row_block, adapter_down_weight, preferred_element_type=jnp.float32
    ).astype(jnp.bfloat16)
    down_sum, up_sum = lax.psum(
        adapter_terms(hidden_row_block, low_rank_rows, value_result, adapter_up_weight),
        ("dp", "ctx"),
    )
    adapter_factor = adapter_scale / (log_batch * segment_list)
    return (
        query_out[None, None],
        key_out[None, None],
        value_result[None, None],
        down_sum * adapter_factor,
        up_sum * adapter_factor,
    )


def solution(mesh):
    placed = (
        P("dp", "ctx", None, None),
        P("dp", "ctx", None, None),
        P("dp", "ctx", None, None),
        P("dp", "ctx", None, None),
        P("dp", "ctx", None, None),
        P(),
        P(),
        P("dp", "ctx"),
    )
    return jax.shard_map(
        per_device,
        mesh=mesh,
        in_specs=placed,
        out_specs=(
            P("dp", "ctx", None, None),
            P("dp", "ctx", None, None),
            P("dp", "ctx", None, None),
            P(),
            P(),
        ),
        check_vma=False,
    )
```

profile of v0, /device:TPU:23, one launch (start us, length us, event | category | flops | bytes accessed | tf_op | source)
XLA Modules:
  0.0 690.2 jit_solution(10573385685993678899)
XLA Ops:
  12.5 56.8 %all-gather.1 = bf16[1,1,800,512]{3,1,0,2:T(2,128)(2,1)S(1)} all-gather(bf16[1,1,50,512]{3,1,0,2:T(2,128)(2,1)S(1)} %copy.106), channel_id=3, replica_groups=mesh['dp'=32,'ctx'=16] {'ctx'}, dimensions={2}, use_global_device_ids=true | all-gather | bytes 870400 | tf_op jit(solution)/shard_map/all_gather | solution.py:84
  69.5 58.1 %all-gather = bf16[1,1,800,512]{3,1,0,2:T(2,128)(2,1)S(1)} all-gather(bf16[1,1,50,512]{3,1,0,2:T(2,128)(2,1)S(1)} %copy.105), channel_id=2, replica_groups=mesh['dp'=32,'ctx'=16] {'ctx'}, dimensions={2}, use_global_device_ids=true | all-gather | bytes 870400 | tf_op jit(solution)/shard_map/all_gather | solution.py:83
  127.8 1.7 fusion.48
  129.5 1.6 fusion.52
  131.1 1.7 fusion.61
  132.8 1.6 fusion.44
  134.7 3.7 fusion.6
  138.4 2.1 convolution_bitcast_fusion.2
  140.5 1.8 fusion.8
  144.6 4.1 fusion.2
  148.7 2.9 convolution_bitcast_fusion.1
  151.6 1.8 fusion.4
  154.6 4.3 fusion.10
  158.9 2.9 convolution_bitcast_fusion.3
  161.8 1.8 fusion.12
  165.8 4.2 fusion.14
  170.0 2.1 convolution_bitcast_fusion.4
  172.2 2.0 fusion.16
  175.7 1.9 pad_maximum_fusion
  177.5 77.3 %fusion.89 = (f32[56,512]{1,0:T(8,128)}, f32[56,512]{1,0:T(8,128)}) fusion(f32[800,512]{1,0:T(8,128)} %get-tuple-element.26, f32[800,512]{1,0:T(8,128)} %get-tuple-element.25), kind=kCustom, calls=%all-reduce-scatter.2 | all-reduce-scatter fusion | flops 917505 | bytes 3508224
  254.8 2.0 collective-permute-start.2
  258.4 1.9 collective-permute-start.3
  260.3 1.9 collective-permute-start
  263.8 12.0 %collective-permute-start.1 = (f32[34,512]{1,0:T(8,128)}, f32[34,512]{1,0:T(8,128)}, u32[]{:S(2)}, u32[]{:S(2)}) collective-permute-start(f32[34,512]{1,0:T(8,128)} %slice.106), channel_id=1, source_target_pairs={{0,2},{1,3},{2,4},{3,5},{4,6},{5,7},{6,8},{7,9},{8,10},{9,11},{10,... | collective-permute-start | bytes 208904
  275.7 2.2 fusion.24
  283.8 1.7 copy.75
  287.4 1.8 pad_maximum_fusion.6
  289.3 2.8 concatenate.44
  293.7 2.8 concatenate.45
  298.6 116.7 %psum.15 = f32[16,512]{1,0:T(8,128)S(1)} all-reduce(f32[16,512]{1,0:T(8,128)S(1)} %fusion.26), channel_id=1, replica_groups=mesh['dp'=32,'ctx'=16] {'dp','ctx'}, use_global_device_ids=true, to_apply=%region_11.12 | all-reduce | flops 8192 | bytes 65536 | tf_op jit(solution)/shard_map/psum | solution.py:126
  417.1 264.6 %all-reduce.7.cloned.1.call-done = f32[4096,16]{0,1:T(8,128)} async-done(((f32[4096,16]{0,1:T(8,128)}), f32[4096,16]{0,1:T(8,128)}) %all-reduce.7.cloned.1.call-update) | async-done | bytes 262160 | tf_op jit(solution)/shard_map/psum | solution.py:126
  681.7 1.7 broadcast_multiply_fusion
  (131 shorter events, 27.7 us)
Async XLA Ops:
  7.2 290.9 %copy-start = (bf16[1,1,128,4096]{3,2,1,0:T(8,128)(2,1)S(1)}, bf16[1,1,128,4096]{3,2,1,0:T(8,128)(2,1)}, u32[]{:S(2)}) copy-start(bf16[1,1,128,4096]{3,2,1,0:T(8,128)(2,1)} %param.12) | copy-start | bytes 3145732
  7.2 4.9 copy-start.31
  7.2 674.5 %all-reduce.7.cloned.1.call-start = ((), (), s32[]{:S(2)}) async-start(), calls=%async_computation | async-start | bytes 524288 | tf_op jit(solution)/shard_map/psum | solution.py:126
  12.1 132.5 %copy-start.34 = (bf16[128,512]{0,1:T(8,128)(2,1)}, bf16[128,512]{0,1:T(8,128)(2,1)S(1)}, u32[]{:S(2)}) copy-start(bf16[128,512]{0,1:T(8,128)(2,1)S(1)} %get-tuple-element.14) | copy-start | bytes 393220
  12.5 117.0 %copy-start.26 = (bf16[128,512]{0,1:T(8,128)(2,1)}, bf16[128,512]{0,1:T(8,128)(2,1)S(1)}, u32[]{:S(2)}) copy-start(bf16[128,512]{0,1:T(8,128)(2,1)S(1)} %get-tuple-element.12) | copy-start | bytes 393220
  69.5 58.3 %copy-start.24 = (bf16[1,1,128,512]{3,2,1,0:T(8,128)(2,1)S(1)}, bf16[1,1,128,512]{3,2,1,0:T(8,128)(2,1)}, u32[]{:S(2)}) copy-start(bf16[1,1,128,512]{3,2,1,0:T(8,128)(2,1)} %param.10) | copy-start | bytes 393220
  134.7 9.9 %copy-start.37 = (pred[128,928]{0,1:T(8,128)(4,1)}, pred[128,928]{0,1:T(8,128)(4,1)S(1)}, u32[]{:S(2)}) copy-start(pred[128,928]{0,1:T(8,128)(4,1)S(1)} %pad_add_fusion) | copy-start | bytes 356356
  134.7 9.9 %copy-start.27 = (bf16[928,128,1]{1,0,2:T(8,128)(2,1)}, bf16[928,128,1]{1,0,2:T(8,128)(2,1)S(1)}, u32[]{:S(2)}) copy-start(bf16[928,128,1]{1,0,2:T(8,128)(2,1)S(1)} %fusion.64) | copy-start | bytes 712708
  148.7 2.9 copy-start.8
  148.7 2.9 copy-start.40
  158.9 2.9 copy-start.7
  158.9 2.9 copy-start.41
  161.8 2.8 copy-start.33
  170.0 2.1 copy-start.39
  172.1 3.5 copy-start.14
  172.1 3.1 copy-start.32
  172.1 3.5 copy-start.10
  172.1 3.5 copy-start.12
  172.2 3.5 copy-start.16
  172.2 3.5 copy-start.18
  172.2 3.5 copy-start.20
  254.8 23.1 %copy-start.28 = (bf16[928,128,1]{1,0,2:T(8,128)(2,1)S(1)}, bf16[928,128,1]{1,0,2:T(8,128)(2,1)}, u32[]{:S(2)}) copy-start(bf16[928,128,1]{1,0,2:T(8,128)(2,1)} %copy-done.27) | copy-start | bytes 712708
  254.8 24.1 %copy-start.3 = (bf16[4,128,928]{1,2,0:T(8,128)(2,1)S(1)}, bf16[4,128,928]{1,2,0:T(8,128)(2,1)}, u32[]{:S(2)}) copy-start(bf16[4,128,928]{1,2,0:T(8,128)(2,1)} %copy-done.2) | copy-start | bytes 2850820
  254.8 38.9 %collective-permute-start.2 = (f32[56,512]{1,0:T(8,128)}, f32[56,512]{1,0:T(8,128)}, u32[]{:S(2)}, u32[]{:S(2)}) collective-permute-start(f32[56,512]{1,0:T(8,128)} %get-tuple-element.8), channel_id=1, source_target_pairs={{0,1},{1,2},{2,3},{3,4},{4,5},{5,6},{6,7},{7,8},{8,9},{9,10},{10,1... | collective-permute-start | bytes 344072
  258.4 35.3 %collective-permute-start.3 = (f32[34,512]{1,0:T(8,128)}, f32[34,512]{1,0:T(8,128)}, u32[]{:S(2)}, u32[]{:S(2)}) collective-permute-start(f32[34,512]{1,0:T(8,128)} %slice.107), channel_id=1, source_target_pairs={{0,2},{1,3},{2,4},{3,5},{4,6},{5,7},{6,8},{7,9},{8,10},{9,11},{10,... | collective-permute-start | bytes 208904
  260.3 28.9 %collective-permute-start = (f32[56,512]{1,0:T(8,128)}, f32[56,512]{1,0:T(8,128)}, u32[]{:S(2)}, u32[]{:S(2)}) collective-permute-start(f32[56,512]{1,0:T(8,128)} %get-tuple-element.7), channel_id=1, source_target_pairs={{0,1},{1,2},{2,3},{3,4},{4,5},{5,6},{6,7},{7,8},{8,9},{9,10},{10,1... | collective-permute-start | bytes 344072
  263.8 25.5 %collective-permute-start.1 = (f32[34,512]{1,0:T(8,128)}, f32[34,512]{1,0:T(8,128)}, u32[]{:S(2)}, u32[]{:S(2)}) collective-permute-start(f32[34,512]{1,0:T(8,128)} %slice.106), channel_id=1, source_target_pairs={{0,2},{1,3},{2,4},{3,5},{4,6},{5,7},{6,8},{7,9},{8,10},{9,11},{10,... | collective-permute-start | bytes 208904
  281.0 8.2 %copy-start.11 = (f32[928,128]{1,0:T(8,128)S(1)}, f32[928,128]{1,0:T(8,128)}, u32[]{:S(2)}) copy-start(f32[928,128]{1,0:T(8,128)} %convolution_bitcast_fusion.1) | copy-start | bytes 1425412
  281.0 8.2 %copy-start.13 = (f32[928,128]{1,0:T(8,128)S(1)}, f32[928,128]{1,0:T(8,128)}, u32[]{:S(2)}) copy-start(f32[928,128]{1,0:T(8,128)} %convolution_bitcast_fusion.3) | copy-start | bytes 1425412
  281.0 8.2 %copy-start.15 = (f32[928,128]{1,0:T(8,128)S(1)}, f32[928,128]{1,0:T(8,128)}, u32[]{:S(2)}) copy-start(f32[928,128]{1,0:T(8,128)} %copy-done.14) | copy-start | bytes 1425412
  289.2 8.9 %copy-start.36 = (bf16[4096,16]{0,1:T(8,128)(2,1)S(1)}, bf16[4096,16]{0,1:T(8,128)(2,1)}, u32[]{:S(2)}) copy-start(bf16[4096,16]{0,1:T(8,128)(2,1)} %param.13) | copy-start | bytes 393220
  292.2 123.2 %copy-start.38 = (bf16[16,512]{1,0:T(8,128)(2,1)S(1)}, bf16[16,512]{1,0:T(8,128)(2,1)}, u32[]{:S(2)}) copy-start(bf16[16,512]{1,0:T(8,128)(2,1)} %param.14) | copy-start | bytes 49156
  (15 other events, 25.5 us)
Sparse Core Ops, SparseCore 0:
  416.6 265.0 all-reduce.6
where the time goes:
time: 691 us; the launch traced here: 690 us
  blocking collectives  309 us (45%)
  waiting for transfers between devices  265 us (38%)
  matrix products  43.7 us (6%)
  local copies, waits for them, and re-layouts  23.8 us (3%)
  starting transfers between devices  17.9 us (3%)
  between operations  16 us (2%)
  other arithmetic  15.3 us (2%)
    psum x1, waiting for transfers between devices, per_device(): lax.psum(adapter_terms(hidden_row_block, low_rank_rows, value_result, ada...  265 us
    psum x1, blocking collectives, per_device(): lax.psum(adapter_terms(hidden_row_block, low_rank_rows, value_result, ada...  117 us
    unnamed x1, blocking collectives  77.3 us
    all_gather x1, blocking collectives, per_device(): lax.all_gather(own_keys, 'ctx', axis=0, tiled=True)  58.1 us
    all_gather x1, blocking collectives, per_device(): lax.all_gather(own_values, 'ctx', axis=0, tiled=True)  56.8 us
    unnamed x4, starting transfers between devices  17.8 us
    div x4, matrix products, group_grads(): attend = unnorm / jnp.sum(unnorm, -1, keepdims=True)  16.4 us
    unnamed x95, local copies, waits for them, and re-layouts  16.1 us
  transfers between devices with their start and end apart: 5, of which 1 were waited for; matrix products, arithmetic and copies ran while one was open for 3% of the time, Pallas kernels for 0%

commit v1 on v0

--- a/solution.py
+++ b/solution.py
@@ -124,8 +124,10 @@
         hidden_row_block, adapter_down_weight, preferred_element_type=jnp.float32
     ).astype(jnp.bfloat16)
     down_sum, up_sum = lax.psum(
-        adapter_terms(hidden_row_block, low_rank_rows, value_result, adapter_up_weight),
-        ("dp", "ctx"),
+        lax.psum(
+            adapter_terms(hidden_row_block, low_rank_rows, value_result, adapter_up_weight), "dp"
+        ),
+        "ctx",
     )
     adapter_factor = adapter_scale / (log_batch * segment_list)
     return (

time: 691 us -> 1020 us (1.48)
  the two profiles are of different devices: /device:TPU:23 before, /device:TPU:2 now
where the time goes in v1:
time: 1020 us
  waiting for transfers between devices  485 us (48%)
  blocking collectives  426 us (42%)
  matrix products  44.6 us (4%)
  local copies, waits for them, and re-layouts  23.3 us (2%)
  between operations  16 us (2%)
  other arithmetic  15.3 us (2%)
    psum x1, waiting for transfers between devices, per_device(): lax.psum(adapter_terms(hidden_row_block, low_rank_rows, value_result, ada...  276 us
    psum x1, waiting for transfers between devices, per_device(): lax.psum(lax.psum(adapter_terms(hidden_row_block, low_rank_rows, value_re...  208 us
    psum x1, blocking collectives, per_device(): lax.psum(adapter_terms(hidden_row_block, low_rank_rows, value_result, ada...  114 us
    psum x1, blocking collectives, per_device(): lax.psum(lax.psum(adapter_terms(hidden_row_block, low_rank_rows, value_re...  92.2 us
    unnamed x1, blocking collectives  84.7 us
    all_gather x1, blocking collectives, per_device(): lax.all_gather(own_values, 'ctx', axis=0, tiled=True)  73.4 us
    all_gather x1, blocking collectives, per_device(): lax.all_gather(own_keys, 'ctx', axis=0, tiled=True)  62.4 us
  transfers between devices with their start and end apart: 6, of which 2 were waited for; matrix products, arithmetic and copies ran while one was open for 3% of the time, Pallas kernels for 0%

profile of v1, /device:TPU:2, one launch (start us, length us, event | category | flops | bytes accessed | tf_op | source)
XLA Modules:
  0.0 1019.6 jit_solution(14762377911569580545)
XLA Ops:
  12.4 73.4 %all-gather.1 = bf16[1,1,800,512]{3,1,0,2:T(2,128)(2,1)S(1)} all-gather(bf16[1,1,50,512]{3,1,0,2:T(2,128)(2,1)S(1)} %copy.106), channel_id=3, replica_groups=mesh['dp'=32,'ctx'=16] {'ctx'}, dimensions={2}, use_global_device_ids=true | all-gather | bytes 870400 | tf_op jit(solution)/shard_map/all_gather | solution.py:84
  86.0 62.4 %all-gather = bf16[1,1,800,512]{3,1,0,2:T(2,128)(2,1)S(1)} all-gather(bf16[1,1,50,512]{3,1,0,2:T(2,128)(2,1)S(1)} %copy.105), channel_id=2, replica_groups=mesh['dp'=32,'ctx'=16] {'ctx'}, dimensions={2}, use_global_device_ids=true | all-gather | bytes 870400 | tf_op jit(solution)/shard_map/all_gather | solution.py:83
  148.7 1.7 fusion.48
  152.0 1.7 fusion.61
  155.6 3.7 fusion.6
  159.3 2.1 convolution_bitcast_fusion.2
  161.4 1.8 fusion.8
  165.4 4.1 fusion.2
  169.5 2.9 convolution_bitcast_fusion.1
  172.5 1.8 fusion.4
  175.5 4.3 fusion.10
  179.8 2.9 convolution_bitcast_fusion.3
  182.7 1.8 fusion.12
  186.6 4.2 fusion.14
  190.9 2.1 convolution_bitcast_fusion.4
  193.0 2.0 fusion.16
  196.5 1.9 pad_maximum_fusion
  198.4 84.7 %fusion.89 = (f32[56,512]{1,0:T(8,128)}, f32[56,512]{1,0:T(8,128)}) fusion(f32[800,512]{1,0:T(8,128)} %get-tuple-element.26, f32[800,512]{1,0:T(8,128)} %get-tuple-element.25), kind=kCustom, calls=%all-reduce-scatter.2 | all-reduce-scatter fusion | flops 917505 | bytes 3508224
  283.1 3.6 collective-permute-start.2
  288.2 1.9 collective-permute-start.3
  290.1 1.9 collective-permute-start
  293.6 1.9 collective-permute-start.1
  295.5 2.2 fusion.24
  303.5 1.7 copy.75
  307.1 1.8 pad_maximum_fusion.6
  309.0 2.8 concatenate.45
  313.9 113.9 %psum.30 = f32[16,512]{1,0:T(8,128)S(1)} all-reduce(f32[16,512]{1,0:T(8,128)S(1)} %fusion.26), channel_id=1, replica_groups=mesh['dp'=32,'ctx'=16] {'dp'}, use_global_device_ids=true, to_apply=%region_12.13 | all-reduce | flops 8192 | bytes 65536 | tf_op jit(solution)/shard_map/psum | solution.py:127
  427.8 92.2 %psum.31 = f32[16,512]{1,0:T(8,128)S(1)} all-reduce(f32[16,512]{1,0:T(8,128)S(1)} %psum.30), channel_id=1, replica_groups=mesh['dp'=32,'ctx'=16] {'ctx'}, use_global_device_ids=true, to_apply=%region_13.14 | all-reduce | flops 8192 | bytes 65536 | tf_op jit(solution)/shard_map/psum | solution.py:126
  521.8 2.8 concatenate.44
  525.3 276.4 %all-reduce.8.cloned.1.call-done = f32[4096,16]{0,1:T(8,128)} async-done(((f32[4096,16]{0,1:T(8,128)}), f32[4096,16]{0,1:T(8,128)}) %all-reduce.8.cloned.1.call-update) | async-done | bytes 262160 | tf_op jit(solution)/shard_map/psum | solution.py:127
  803.1 208.0 %all-reduce.10.cloned.1.call-done = f32[4096,16]{0,1:T(8,128)} async-done(((f32[4096,16]{0,1:T(8,128)}), f32[4096,16]{0,1:T(8,128)}) %all-reduce.10.cloned.1.call-update) | async-done | bytes 262160 | tf_op jit(solution)/shard_map/psum | solution.py:126
  1011.1 1.7 broadcast_multiply_fusion
  (133 shorter events, 31.4 us)
Async XLA Ops:
  7.2 305.3 %copy-start = (bf16[1,1,128,4096]{3,2,1,0:T(8,128)(2,1)S(1)}, bf16[1,1,128,4096]{3,2,1,0:T(8,128)(2,1)}, u32[]{:S(2)}) copy-start(bf16[1,1,128,4096]{3,2,1,0:T(8,128)(2,1)} %param.12) | copy-start | bytes 3145732
  7.2 4.9 copy-start.31
  7.2 794.6 %all-reduce.8.cloned.1.call-start = ((), (), s32[]{:S(2)}) async-start(), calls=%async_computation | async-start | bytes 524288 | tf_op jit(solution)/shard_map/psum | solution.py:127
  12.1 153.4 %copy-start.34 = (bf16[128,512]{0,1:T(8,128)(2,1)}, bf16[128,512]{0,1:T(8,128)(2,1)S(1)}, u32[]{:S(2)}) copy-start(bf16[128,512]{0,1:T(8,128)(2,1)S(1)} %get-tuple-element.14) | copy-start | bytes 393220
  12.4 137.9 %copy-start.26 = (bf16[128,512]{0,1:T(8,128)(2,1)}, bf16[128,512]{0,1:T(8,128)(2,1)S(1)}, u32[]{:S(2)}) copy-start(bf16[128,512]{0,1:T(8,128)(2,1)S(1)} %get-tuple-element.12) | copy-start | bytes 393220
  86.0 62.7 %copy-start.24 = (bf16[1,1,128,512]{3,2,1,0:T(8,128)(2,1)S(1)}, bf16[1,1,128,512]{3,2,1,0:T(8,128)(2,1)}, u32[]{:S(2)}) copy-start(bf16[1,1,128,512]{3,2,1,0:T(8,128)(2,1)} %param.10) | copy-start | bytes 393220
  155.5 9.9 copy-start.36
  155.6 9.9 copy-start.27
  169.5 2.9 copy-start.8
  169.5 2.9 copy-start.39
  179.8 2.9 copy-start.7
  179.8 2.9 copy-start.40
  182.6 2.8 copy-start.33
  190.8 2.1 copy-start.38
  192.9 3.5 copy-start.14
  193.0 3.0 copy-start.32
  193.0 3.5 copy-start.10
  193.0 3.5 copy-start.12
  193.0 3.5 copy-start.16
  193.0 3.5 copy-start.18
  193.0 3.5 copy-start.20
  283.0 14.6 %copy-start.28 = (bf16[928,128,1]{1,0,2:T(8,128)(2,1)S(1)}, bf16[928,128,1]{1,0,2:T(8,128)(2,1)}, u32[]{:S(2)}) copy-start(bf16[928,128,1]{1,0,2:T(8,128)(2,1)} %copy-done.27) | copy-start | bytes 712708
  283.0 15.6 %copy-start.3 = (bf16[4,128,928]{1,2,0:T(8,128)(2,1)S(1)}, bf16[4,128,928]{1,2,0:T(8,128)(2,1)}, u32[]{:S(2)}) copy-start(bf16[4,128,928]{1,2,0:T(8,128)(2,1)} %copy-done.2) | copy-start | bytes 2850820
  283.1 26.0 %collective-permute-start.2 = (f32[56,512]{1,0:T(8,128)}, f32[56,512]{1,0:T(8,128)}, u32[]{:S(2)}, u32[]{:S(2)}) collective-permute-start(f32[56,512]{1,0:T(8,128)} %get-tuple-element.8), channel_id=1, source_target_pairs={{0,1},{1,2},{2,3},{3,4},{4,5},{5,6},{6,7},{7,8},{8,9},{9,10},{10,1... | collective-permute-start | bytes 344072
  288.2 20.8 %collective-permute-start.3 = (f32[34,512]{1,0:T(8,128)}, f32[34,512]{1,0:T(8,128)}, u32[]{:S(2)}, u32[]{:S(2)}) collective-permute-start(f32[34,512]{1,0:T(8,128)} %slice.107), channel_id=1, source_target_pairs={{0,2},{1,3},{2,4},{3,5},{4,6},{5,7},{6,8},{7,9},{8,10},{9,11},{10,... | collective-permute-start | bytes 208904
  290.1 231.7 %collective-permute-start = (f32[56,512]{1,0:T(8,128)}, f32[56,512]{1,0:T(8,128)}, u32[]{:S(2)}, u32[]{:S(2)}) collective-permute-start(f32[56,512]{1,0:T(8,128)} %get-tuple-element.7), channel_id=1, source_target_pairs={{0,1},{1,2},{2,3},{3,4},{4,5},{5,6},{6,7},{7,8},{8,9},{9,10},{10,1... | collective-permute-start | bytes 344072
  293.6 228.2 %collective-permute-start.1 = (f32[34,512]{1,0:T(8,128)}, f32[34,512]{1,0:T(8,128)}, u32[]{:S(2)}, u32[]{:S(2)}) collective-permute-start(f32[34,512]{1,0:T(8,128)} %slice.106), channel_id=1, source_target_pairs={{0,2},{1,3},{2,4},{3,5},{4,6},{5,7},{6,8},{7,9},{8,10},{9,11},{10,... | collective-permute-start | bytes 208904
  300.8 8.2 copy-start.11
  300.8 8.2 copy-start.13
  300.8 8.2 copy-start.15
  309.0 211.0 %copy-start.37 = (bf16[16,512]{1,0:T(8,128)(2,1)S(1)}, bf16[16,512]{1,0:T(8,128)(2,1)}, u32[]{:S(2)}) copy-start(bf16[16,512]{1,0:T(8,128)(2,1)} %param.14) | copy-start | bytes 49156
  521.2 490.0 %all-reduce.10.cloned.1.call-start = ((), (), s32[]{:S(2)}) async-start(), calls=%async_computation.1 | async-start | bytes 524288 | tf_op jit(solution)/shard_map/psum | solution.py:126
  (15 other events, 25.4 us)
Sparse Core Ops, SparseCore 0:
  521.3 280.4 all-reduce.7
  804.9 206.1 all-reduce.9
